TPU v7x, 32 devices: a whole 2x2x4 slice. The times are simulated.
32 devices in a mesh: ctx: 16 (over z, y, x), tp: 2 (over core).
Axes of the slice: x: 2, y: 2, z: 4, core: 2. Of those that a mesh axis runs over, the one named last changes fastest.
Arguments:
- x_act: bfloat16 [4096, 8192], P('ctx', 'tp'), may hold values from -0.119628906 to 0.119628906
- b_proj: bfloat16 [4096, 128], P('ctx'), may hold values from -0.5 to 0.5
- c_proj: bfloat16 [4096, 128], P('ctx'), may hold values from -0.5 to 0.5
- dt_raw: bfloat16 [4096, 128], P('ctx', 'tp'), may hold values from -3 to 3
- a_log: float32 [128], P('tp'), may hold values from -12 to -2
- d_skip: float32 [128], P('tp'), may hold values from 0.5 to 2
- grad_out: bfloat16 [4096, 8192], P('ctx', 'tp'), may hold values from -6 to 6
Outputs:
- grad_x: bfloat16 [4096, 8192], P('ctx', 'tp')
- grad_b: float32 [4096, 128], P('ctx')
- grad_c: float32 [4096, 128], P('ctx')
- grad_dt: bfloat16 [4096, 128], P('ctx', 'tp')
All inputs are finite; a program needn't handle non-finite values.
Results may differ from a plain program's by a relative error of at most 0.001.
Values may be sent and summed in bfloat16 or wider, within the bound.
No kernel may reach another device: no remote copies, remote signals or barrier semaphores. Data moves between devices by JAX's collectives and lax.ppermute only.
A program may use at most 192 MiB of HBM per device.

v0:
```python
from functools import partial

import jax
import jax.numpy as jnp
from jax import lax
from jax.sharding import PartitionSpec as P

BLOCK = 256


precise = lax.Precision.HIGHEST


def head_forward(x_head, b_rows, c_rows, raw_step, log_rate, skip_gain, start_state, block_len):
    length, head_width = x_head.shape
    blocks = length // block_len
    step_size = jax.nn.softplus(raw_step)
    decay_rates = -jnp.exp(log_rate) * step_size
    row_index = lax.broadcasted_iota(jnp.int32, (block_len, block_len), 0)
    col_index = lax.broadcasted_iota(jnp.int32, (block_len, block_len), 1)
    lower_mask = row_index >= col_index
    running = jnp.dot(
        decay_rates.reshape(blocks, block_len), lower_mask.astype(jnp.float32).T, precision=precise
    )
    between = jnp.where(lower_mask[None], running[:, :, None] - running[:, None, :], -1e30)
    x_blocks = x_head.reshape(blocks, block_len, head_width)
    b_blocks = b_rows.reshape(blocks, block_len, -1)
    c_blocks = c_rows.reshape(blocks, block_len, -1)
    s_blocks = step_size.reshape(blocks, block_len)
    scores = (
        jnp.einsum("kin,kjn->kij", c_blocks, b_blocks, precision=precise)
        * jnp.exp(between)
        * s_blocks[:, None, :]
    )
    output = jnp.einsum("kij,kjp->kip", scores, x_blocks, precision=precise)
    closing = running[:, -1]
    weighted = (jnp.exp(closing[:, None] - running) * s_blocks)[:, :, None] * x_blocks
    states = jnp.einsum("kjp,kjn->kpn", weighted, b_blocks, precision=precise)
    block_rows = lax.broadcasted_iota(jnp.int32, (blocks, blocks), 0)
    block_cols = lax.broadcasted_iota(jnp.int32, (blocks, blocks), 1)
    through = jnp.dot((block_rows >= block_cols).astype(jnp.float32), closing, precision=precise)
    before = through - closing
    carry_weight = jnp.exp(
        jnp.where(block_rows > block_cols, before[:, None] - through[None, :], -1e30)
    )
    entering = (
        jnp.einsum("kj,jpn->kpn", carry_weight, states, precision=precise)
        + jnp.exp(before)[:, None, None] * start_state[None]
    )
    reading = jnp.exp(running)[:, :, None] * c_blocks
    output = output + jnp.einsum("kin,kpn->kip", reading, entering, precision=precise)
    output = output.reshape(length, head_width) + skip_gain * x_head
    final_state = (
        jnp.einsum("j,jpn->pn", jnp.exp(through[-1] - through), states, precision=precise)
        + jnp.exp(through[-1]) * start_state
    )
    return (output, final_state)


N_CHUNKS = 1


def chunk_backward(x_seq, g_seq, raw_seq, b_rows, c_rows, rate, gain):
    length = x_seq.shape[0]
    heads = raw_seq.shape[1]
    head_width = x_seq.shape[1] // heads
    runner = partial(head_forward, block_len=BLOCK)
    mapped = jax.vmap(runner, in_axes=(0, None, None, 0, 0, 0, 0))
    x_heads = x_seq.astype(jnp.float32).reshape(length, heads, head_width).transpose(1, 0, 2)
    g_heads = g_seq.astype(jnp.float32).reshape(length, heads, head_width).transpose(1, 0, 2)
    raw_heads = raw_seq.astype(jnp.float32).T
    anchor = jnp.zeros((heads, head_width, b_rows.shape[1]), jnp.float32)

    def forward(x_val, b_val, c_val, raw_val):
        return mapped(x_val, b_val, c_val, raw_val, rate, gain, anchor)[0]

    _, pullback = jax.vjp(forward, x_heads, b_rows, c_rows, raw_heads)
    grad_xh, grad_b_all, grad_c_all, grad_raw = pullback(g_heads)
    x_back = grad_xh.transpose(1, 0, 2).reshape(length, heads * head_width).astype(jnp.bfloat16)
    raw_back = grad_raw.T.astype(jnp.bfloat16)
    return x_back, raw_back, grad_b_all, grad_c_all


def local(x_act, b_proj, c_proj, dt_raw, a_log, d_skip, grad_out):
    rows = x_act.shape[0]
    heads_here = dt_raw.shape[1]
    head_width = x_act.shape[1] // heads_here
    state = b_proj.shape[1]
    owners = lax.axis_size("ctx")
    per_owner = heads_here // owners
    chunks = N_CHUNKS if per_owner % N_CHUNKS == 0 else 1
    per_chunk = per_owner // chunks
    me = lax.axis_index("ctx")
    half = lax.axis_index("tp")

    first_head = me * per_owner
    rate_own = lax.dynamic_slice_in_dim(a_log, first_head, per_owner)
    gain_own = lax.dynamic_slice_in_dim(d_skip, first_head, per_owner)

    x4 = x_act.reshape(rows, owners, per_owner, head_width)
    g4 = grad_out.reshape(rows, owners, per_owner, head_width)
    r3 = dt_raw.reshape(rows, owners, per_owner)
    x_parts, raw_parts = [], []
    grad_b_all = None
    grad_c_all = None
    for c in range(chunks):
        sl = slice(c * per_chunk, (c + 1) * per_chunk)
        width = per_chunk * head_width
        pieces = [x4[:, :, sl, :].reshape(rows, owners, width), g4[:, :, sl, :].reshape(rows, owners, width)]
        if c == 0:
            own_proj = jnp.where(half == 0, b_proj, c_proj)
            pieces.append(jnp.broadcast_to(own_proj[:, None, :], (rows, owners, state)))
        xg = jnp.concatenate(pieces, axis=2)
        xg_seq = lax.all_to_all(xg, "ctx", split_axis=1, concat_axis=0, tiled=True).reshape(rows * owners, -1)
        if c == 0:
            own_seq = xg_seq[:, 2 * width :]
            other_seq = lax.ppermute(own_seq, "tp", [(0, 1), (1, 0)])
            b_rows = jnp.where(half == 0, own_seq, other_seq).astype(jnp.float32)
            c_rows = jnp.where(half == 0, other_seq, own_seq).astype(jnp.float32)
        raw_seq = lax.all_to_all(r3[:, :, sl], "ctx", split_axis=1, concat_axis=0, tiled=True).reshape(
            rows * owners, per_chunk
        )
        x_back, raw_back, gb, gc = chunk_backward(
            xg_seq[:, :width], xg_seq[:, width : 2 * width], raw_seq, b_rows, c_rows, rate_own[sl], gain_own[sl]
        )
        x_parts.append(
            lax.all_to_all(x_back, "ctx", split_axis=0, concat_axis=1, tiled=True).reshape(rows, owners, 1, width)
        )
        raw_parts.append(
            lax.all_to_all(raw_back, "ctx", split_axis=0, concat_axis=1, tiled=True).reshape(rows, owners, 1, per_chunk)
        )
        grad_b_all = gb if grad_b_all is None else grad_b_all + gb
        grad_c_all = gc if grad_c_all is None else grad_c_all + gc
    grad_x = jnp.concatenate(x_parts, axis=2).reshape(rows, owners * per_owner * head_width)
    grad_dt = jnp.concatenate(raw_parts, axis=2).reshape(rows, heads_here)

    is_first = half == 0
    send = jnp.where(is_first, grad_c_all, grad_b_all)
    keep = jnp.where(is_first, grad_b_all, grad_c_all)
    mine = keep + lax.ppermute(send, "tp", [(0, 1), (1, 0)])
    parts = lax.all_to_all(mine.reshape(owners, rows, state), "ctx", split_axis=0, concat_axis=0, tiled=True)
    mine = parts.sum(axis=0)
    other = lax.ppermute(mine, "tp", [(0, 1), (1, 0)])
    grad_b = jnp.where(is_first, mine, other)
    grad_c = jnp.where(is_first, other, mine)
    return (grad_x, grad_b, grad_c, grad_dt)


def solution(mesh):
    in_specs = (
        P("ctx", "tp"),
        P("ctx", None),
        P("ctx", None),
        P("ctx", "tp"),
        P("tp"),
        P("tp"),
        P("ctx", "tp"),
    )
    out_specs = (P("ctx", "tp"), P("ctx", None), P("ctx", None), P("ctx", "tp"))
    return jax.shard_map(local, mesh=mesh, in_specs=in_specs, out_specs=out_specs, check_vma=False)
```

profile of v0, /device:TPU:12, one launch (start us, length us, event | category | flops | bytes accessed | tf_op | source)
XLA Modules:
  0.0 367.0 jit_solution(17081317046815837315)
XLA Ops:
  2.0 7.2 %all-to-all-start.1 = ((bf16[256,16,4]{0,2,1:T(4,128)(2,1)}), bf16[256,16,4]{0,2,1:T(4,128)(2,1)S(1)}, u32[]{:S(2)}, u32[]{:S(2)}) async-start(bf16[256,16,4]{0,2,1:T(4,128)(2,1)} %reshape.132), calls=%async_computation.1 | async-start | bytes 65536 | tf_op jit(solution)/shard_map/all_to_all | solution.py:120
  10.2 3.3 copy.77
  13.4 4.1 %copy.78 = bf16[256,4096]{0,1:T(8,128)(2,1)} copy(bf16[256,4096]{1,0:T(8,128)(2,1)} %param.13) | data formatting | bytes 4194304 | tf_op args[6]
  17.6 4.3 %pad_maximum_fusion = bf16[256,16,640]{0,2,1:T(8,128)(2,1)} fusion(bf16[256,16,128]{0,2,1:T(8,128)(2,1)S(1)} %broadcast_in_dim.52, bf16[256,16,256]{0,2,1:T(8,128)(2,1)} %bitcast.185, bf16[256,16,256]{0,2,1:T(8,128)(2,1)S(1)} %bitcast.184), kind=kLoop, calls=%fused_computation.16 | loop fusion | flops 15728640 | bytes 10485760 | tf_op jit(solution)/shard_map/concatenate | solution.py:113
  21.9 7.0 %all-to-all-start = ((bf16[256,16,640]{0,2,1:T(8,128)(2,1)}), bf16[256,16,640]{0,2,1:T(8,128)(2,1)}, u32[]{:S(2)}, u32[]{:S(2)}) async-start(bf16[256,16,640]{0,2,1:T(8,128)(2,1)} %pad_maximum_fusion), calls=%async_computation | async-start | bytes 10485760 | tf_op jit(solution)/shard_map/all_to_all | solution.py:114
  31.1 114.3 %all-to-all-done = bf16[256,16,640]{0,2,1:T(8,128)(2,1)} async-done(((bf16[256,16,640]{0,2,1:T(8,128)(2,1)}), bf16[256,16,640]{0,2,1:T(8,128)(2,1)}, u32[]{:S(2)}, u32[]{:S(2)}) %all-to-all-start) | async-done | bytes 5242912 | tf_op jit(solution)/shard_map/all_to_all | solution.py:114
  145.4 7.8 %copy.80 = bf16[16,256,1,640]{3,1,0,2:T(8,128)(2,1)} copy(bf16[16,256,1,640]{1,3,0,2:T(8,128)(2,1)} %bitcast.3) | data formatting | bytes 10485760 | tf_op jit(solution)/shard_map/all_to_all | solution.py:114
  154.6 4.5 %fusion.112 = (bf16[4096,256]{1,0:T(8,128)(2,1)}, bf16[4096,256]{1,0:T(8,128)(2,1)}) fusion(bf16[4096,640]{1,0:T(8,128)(2,1)} %bitcast.172), kind=kLoop, calls=%fused_computation.132 | loop fusion | bytes 8388608 | tf_op jit(solution)/shard_map/slice | solution.py:124
  162.0 4.1 %copy.81 = bf16[4096,256]{0,1:T(8,128)(2,1)} copy(bf16[4096,256]{1,0:T(8,128)(2,1)} %get-tuple-element.25) | data formatting | bytes 4194304 | tf_op jit(solution)/shard_map/slice | solution.py:124
  174.1 6.0 %multiply_reduce_fusion.4 = (f32[4,16]{1,0:T(4,128)}, f32[4,16,64,128]{3,2,1,0:T(8,128)S(1)}) fusion(f32[16,256,128]{1,2,0:T(8,128)S(1)} %copy-done.9, f32[4,16,256]{2,1,0:T(8,128)S(1)} %get-tuple-element.36, bf16[4,8,16,8,256]{4,3,2,1,0:T(8,128)(2,1)S(1)} %bitcast.174), kind=kOutput, calls=%fused_computation.41 | convolution fusion | flops 1613758464 | bytes 6357248 | tf_op jit(solution)/shard_map/transpose(jvp(vmap(kin,kpn->kip)))/dot_general | solution.py:51
  180.0 3.2 fusion.44
  183.2 4.5 %fusion.10 = (f32[4,16,256]{2,0,1:T(4,128)S(1)}, f32[16,4,64,256]{3,2,1,0:T(8,128)}) fusion(bf16[4,8,16,8,256]{4,3,2,1,0:T(8,128)(2,1)S(1)} %bitcast.163, bf16[16,256,128,1]{2,1,3,0:T(8,128)(2,1)S(1)} %bitcast.168, f32[16,4,64,128]{3,0,2,1:T(8,128)S(1)} %fusion.44), kind=kOutput, calls=%fused_computation.19 | convolution fusion | flops 1613742080 | bytes 9502720 | tf_op jit(solution)/shard_map/transpose(jvp(vmap(kjp,kjn->kpn)))/dot_general | solution.py:38
  187.7 16.4 %fusion.5 = (f32[4,16,256]{2,1,0:T(8,128)}, f32[4,16,256]{2,1,0:T(8,128)}, f32[4,16,256]{2,1,0:T(8,128)S(1)}, f32[16,256,256]{2,1,0:T(8,128)}, f32[4,16,256,256]{3,2,1,0:T(8,128)}) fusion(f32[4,16,256]{2,1,0:T(8,128)S(1)} %bitcast.198, f32[4,16,256]{2,1,0:T(8,128)S(1)} %get-tuple-element.37, f32[16,256,256]{2,1,0:T(8,128)S(1)} %fusion.114, ...), kind=kOutput, calls=%fused_computation.9 | convolution fusion | flops 594493440 | bytes 29753344 | tf_op jit(solution)/shard_map/transpose(jvp(vmap(kij,kjp->kip)))/dot_general | solution.py:35
  204.9 8.6 %fusion.9 = f32[16,256,128,1]{2,1,3,0:T(8,128)} fusion(f32[4,16,256]{2,0,1:T(4,128)S(1)} %copy.82, f32[16,4,64,128]{3,0,2,1:T(8,128)S(1)} %fusion.44, bf16[4,8,16,8,256]{4,3,2,1,0:T(8,128)(2,1)S(1)} %bitcast.165), kind=kOutput, calls=%fused_computation.18 | convolution fusion | flops 1612709888 | bytes 6356992 | tf_op jit(solution)/shard_map/transpose(jvp(vmap(kjp,kjn->kpn)))/dot_general | solution.py:38
  220.2 6.6 %multiply_reduce_fusion.2 = (f32[4,16,256]{2,1,0:T(8,128)}, f32[16,256,128]{1,2,0:T(8,128)}) fusion(f32[16,256,128]{1,2,0:T(8,128)S(1)} %copy-done.9, f32[4,16,256]{2,1,0:T(8,128)S(1)} %copy-done.11, f32[4,16,64,128]{3,1,2,0:T(8,128)S(1)} %fusion.47, bf16[4,8,16,8,256]{4,3,2,1,0:T(8,128)(2,1)S(1)} %bitcast.176), kind=kOutput, calls=%fused_computation.10 | convolution fusion | flops 1618460672 | bytes 8519680 | tf_op jit(solution)/shard_map/transpose(jvp(vmap(kin,kpn->kip)))/dot_general | solution.py:51
  228.8 4.5 %convolution_add_fusion = f32[16,256,128]{2,1,0:T(8,128)S(1)} fusion(f32[16,256,128]{2,1,0:T(8,128)S(1)} %copy.102, f32[16,256,256]{2,1,0:T(8,128)} %get-tuple-element.15, bf16[16,256,128]{2,1,0:T(8,128)(2,1)S(1)} %bitcast.170), kind=kOutput, calls=%fused_computation.56 | convolution fusion | flops 1611137024 | bytes 9437184 | tf_op jit(solution)/shard_map/transpose(jvp(vmap(kin,kjn->kij)))/dot_general | solution.py:31
  233.3 4.9 %broadcast_select_fusion.1 = (f32[16,256,128]{2,1,0:T(8,128)S(1)}, f32[16,256,128]{2,1,0:T(8,128)}) fusion(f32[16,256,128]{2,1,0:T(8,128)S(1)} %convolution_add_fusion, pred[]{:T(512)S(6)} %eq.14, f32[16,256,256]{2,1,0:T(8,128)S(1)} %copy-done.4, bf16[16,256,128]{2,1,0:T(8,128)(2,1)S(1)} %bitcast.182, f32[16,256,128,1]{2,1,3,0:T(8,128)S(1)} %copy-done.8), kind=kOutput, calls=%fused_computation.70 | convolution fusion | flops 1612185600 | bytes 13631489 | tf_op jit(solution)/shard_map/transpose(jvp(vmap(kin,kjn->kij)))/dot_general | solution.py:31
  238.8 5.3 %fusion.111 = (f32[4,16]{1,0:T(4,128)S(1)}, f32[4,16]{1,0:T(4,128)S(1)}) fusion(f32[4,16]{1,0:T(4,128)S(1)} %get-tuple-element.38, f32[4,16]{1,0:T(4,128)S(1)} %get-tuple-element.21, f32[16,4,64,128]{3,2,1,0:T(8,128)S(1)} %copy-done.1, f32[4,16,64,128]{3,2,1,0:T(8,128)S(1)} %copy-done.7, pred[16,16]{1,0:T(8,128)(4,1)S(1)} %iota_compare_fusion.6), kind=kOutput, calls=%fused_computation.131 | convolution fusion | flops 100669312 | bytes 4195584 | tf_op jit(solution)/shard_map/transpose(jvp(vmap(kj,jpn->kpn)))/dot_general | solution.py:47
  245.5 5.6 %all-to-all-start.4 = ((bf16[16,256,4]{1,2,0:T(4,128)(2,1)}), bf16[16,256,4]{1,2,0:T(4,128)(2,1)S(1)}, u32[]{:S(2)}, u32[]{:S(2)}) async-start(bf16[16,256,4]{1,2,0:T(4,128)(2,1)} %bitcast.41), calls=%async_computation.4 | async-start | bytes 65536 | tf_op jit(solution)/shard_map/all_to_all | solution.py:130
  256.4 7.0 %all-to-all-start.3 = ((f32[16,256,128]{2,1,0:T(8,128)}), f32[16,256,128]{2,1,0:T(8,128)}, u32[]{:S(2)}, u32[]{:S(2)}) async-start(f32[16,256,128]{2,1,0:T(8,128)} %bitcast.183), calls=%async_computation.3 | async-start | bytes 4194304 | tf_op jit(solution)/shard_map/all_to_all | solution.py:141
  263.4 10.8 %fusion.12 = f32[16,4,8,8,256]{4,3,2,1,0:T(8,128)S(1)} fusion(f32[16,4,64,256]{3,2,1,0:T(8,128)} %get-tuple-element.40, f32[4,16,256]{2,0,1:T(4,128)S(1)} %copy.82, bf16[4,8,16,8,256]{4,3,2,1,0:T(8,128)(2,1)S(1)} %bitcast.177, f32[4,16,256,256]{3,2,1,0:T(8,128)} %get-tuple-element.26), kind=kOutput, calls=%fused_computation.22 | convolution fusion | flops 3223322624 | bytes 27328512 | tf_op jit(solution)/shard_map/transpose(jvp(vmap(kij,kjp->kip)))/dot_general | solution.py:35
  278.2 32.7 %all-to-all-done.3 = f32[16,256,128]{2,1,0:T(8,128)} async-done(((f32[16,256,128]{2,1,0:T(8,128)}), f32[16,256,128]{2,1,0:T(8,128)}, u32[]{:S(2)}, u32[]{:S(2)}) %all-to-all-start.3) | async-done | bytes 2097184 | tf_op jit(solution)/shard_map/all_to_all | solution.py:141
  310.8 4.7 %all-to-all-start.2 = ((bf16[16,256,256]{1,2,0:T(8,128)(2,1)}), bf16[16,256,256]{1,2,0:T(8,128)(2,1)S(1)}, u32[]{:S(2)}, u32[]{:S(2)}) async-start(bf16[16,256,256]{1,2,0:T(8,128)(2,1)} %copy.92), calls=%async_computation.2 | async-start | bytes 4194304 | tf_op jit(solution)/shard_map/all_to_all | solution.py:127
  317.9 45.2 %all-to-all-done.2 = bf16[16,256,256]{1,2,0:T(8,128)(2,1)S(1)} async-done(((bf16[16,256,256]{1,2,0:T(8,128)(2,1)}), bf16[16,256,256]{1,2,0:T(8,128)(2,1)S(1)}, u32[]{:S(2)}, u32[]{:S(2)}) %all-to-all-start.2) | async-done | bytes 2097184 | tf_op jit(solution)/shard_map/all_to_all | solution.py:127
  (93 shorter events, 43.1 us)
Async XLA Ops:
  2.0 19.9 %all-to-all-start.1 = ((bf16[256,16,4]{0,2,1:T(4,128)(2,1)}), bf16[256,16,4]{0,2,1:T(4,128)(2,1)S(1)}, u32[]{:S(2)}, u32[]{:S(2)}) async-start(bf16[256,16,4]{0,2,1:T(4,128)(2,1)} %reshape.132), calls=%async_computation.1 | async-start | bytes 65536 | tf_op jit(solution)/shard_map/all_to_all | solution.py:120
  21.9 7.1 %copy-start.20 = (f32[64]{0:T(128)S(1)}, f32[64]{0:T(128)}, u32[]{:S(2)}) copy-start(f32[64]{0:T(128)} %param.11) | copy-start | bytes 772
  21.9 123.5 %all-to-all-start = ((bf16[256,16,640]{0,2,1:T(8,128)(2,1)}), bf16[256,16,640]{0,2,1:T(8,128)(2,1)}, u32[]{:S(2)}, u32[]{:S(2)}) async-start(bf16[256,16,640]{0,2,1:T(8,128)(2,1)} %pad_maximum_fusion), calls=%async_computation | async-start | bytes 10485760 | tf_op jit(solution)/shard_map/all_to_all | solution.py:114
  30.1 143.5 %copy-start.10 = (f32[4,16,256]{2,1,0:T(8,128)}, f32[4,16,256]{2,1,0:T(8,128)S(1)}, u32[]{:S(2)}) copy-start(f32[4,16,256]{2,1,0:T(8,128)S(1)} %get-tuple-element.36) | copy-start | bytes 196612
  154.5 11.6 %collective-permute-start = (bf16[4096,128]{1,0:T(8,128)(2,1)S(1)}, bf16[4096,128]{1,0:T(8,128)(2,1)}, u32[]{:S(2)}, u32[]{:S(2)}) collective-permute-start(bf16[4096,128]{1,0:T(8,128)(2,1)S(1)} %slice.18), channel_id=1, source_target_pairs={{0,1},{1,0},{2,3},{3,2},{4,5},{5,4},{6,7},{7,6},{8,9},{9,8},{10,11... | collective-permute-start | bytes 3145736 | tf_op jit(solution)/shard_map/ppermute | solution.py:117
  183.2 4.5 %copy-start.15 = (f32[1,4,16,256]{3,2,1,0:T(8,128)S(1)}, f32[1,4,16,256]{3,2,1,0:T(8,128)}, u32[]{:S(2)}) copy-start(f32[1,4,16,256]{3,2,1,0:T(8,128)} %copy.237) | copy-start | bytes 196612
  228.7 4.5 %copy-start.4 = (f32[16,256,256]{2,1,0:T(8,128)S(1)}, f32[16,256,256]{2,1,0:T(8,128)}, u32[]{:S(2)}) copy-start(f32[16,256,256]{2,1,0:T(8,128)} %get-tuple-element.15) | copy-start | bytes 12582916
  228.8 4.5 %copy-start.5 = (bf16[4096,128]{1,0:T(8,128)(2,1)S(1)}, bf16[4096,128]{1,0:T(8,128)(2,1)}, u32[]{:S(2)}) copy-start(bf16[4096,128]{1,0:T(8,128)(2,1)} %get-tuple-element.22) | copy-start | bytes 3145732
  228.8 4.5 %copy-start.8 = (f32[16,256,128,1]{2,1,3,0:T(8,128)S(1)}, f32[16,256,128,1]{2,1,3,0:T(8,128)}, u32[]{:S(2)}) copy-start(f32[16,256,128,1]{2,1,3,0:T(8,128)} %fusion.9) | copy-start | bytes 6291460
  233.3 5.5 %copy-start.1 = (f32[16,4,64,128]{3,2,1,0:T(8,128)S(1)}, f32[16,4,64,128]{3,2,1,0:T(8,128)}, u32[]{:S(2)}) copy-start(f32[16,4,64,128]{3,2,1,0:T(8,128)} %copy-done) | copy-start | bytes 6291460
  233.3 5.5 %copy-start.7 = (f32[4,16,64,128]{3,2,1,0:T(8,128)S(1)}, f32[4,16,64,128]{3,2,1,0:T(8,128)}, u32[]{:S(2)}) copy-start(f32[4,16,64,128]{3,2,1,0:T(8,128)} %copy-done.6) | copy-start | bytes 6291460
  238.2 5.9 %copy-start.17 = (f32[4,16]{1,0:T(4,128)S(1)}, f32[4,16]{1,0:T(4,128)}, u32[]{:S(2)}) copy-start(f32[4,16]{1,0:T(4,128)} %get-tuple-element.31) | copy-start | bytes 772
  238.2 5.9 %copy-start.22 = (f32[4,16]{1,0:T(4,128)S(1)}, f32[4,16]{1,0:T(4,128)}, u32[]{:S(2)}) copy-start(f32[4,16]{1,0:T(4,128)} %get-tuple-element.41) | copy-start | bytes 772
  238.2 6.1 %copy-start.12 = (f32[4,16,256]{2,1,0:T(8,128)S(1)}, f32[4,16,256]{2,1,0:T(8,128)}, u32[]{:S(2)}) copy-start(f32[4,16,256]{2,1,0:T(8,128)} %get-tuple-element.12) | copy-start | bytes 196612
  238.2 6.1 %copy-start.13 = (f32[4,16,256]{2,1,0:T(8,128)S(1)}, f32[4,16,256]{2,1,0:T(8,128)}, u32[]{:S(2)}) copy-start(f32[4,16,256]{2,1,0:T(8,128)} %get-tuple-element.13) | copy-start | bytes 196612
  238.2 6.1 %copy-start.14 = (f32[4,16,256]{2,1,0:T(8,128)S(1)}, f32[4,16,256]{2,1,0:T(8,128)}, u32[]{:S(2)}) copy-start(f32[4,16,256]{2,1,0:T(8,128)} %get-tuple-element.16) | copy-start | bytes 196612
  238.3 6.5 %copy-start.19 = (f32[4]{0:T(128)S(1)}, f32[4]{0:T(128)}, u32[]{:S(2)}) copy-start(f32[4]{0:T(128)} %copy-done.18) | copy-start | bytes 52
  238.3 12.9 %collective-permute-start.1 = (f32[4096,128]{1,0:T(8,128)}, f32[4096,128]{1,0:T(8,128)}, u32[]{:S(2)}, u32[]{:S(2)}) collective-permute-start(f32[4096,128]{1,0:T(8,128)} %bitcast.35), channel_id=1, source_target_pairs={{0,1},{1,0},{2,3},{3,2},{4,5},{5,4},{6,7},{7,6},{8,9},{9,8},{10,11... | collective-permute-start | bytes 6291464 | tf_op jit(solution)/shard_map/ppermute | solution.py:140
  245.5 10.9 %all-to-all-start.4 = ((bf16[16,256,4]{1,2,0:T(4,128)(2,1)}), bf16[16,256,4]{1,2,0:T(4,128)(2,1)S(1)}, u32[]{:S(2)}, u32[]{:S(2)}) async-start(bf16[16,256,4]{1,2,0:T(4,128)(2,1)} %bitcast.41), calls=%async_computation.4 | async-start | bytes 65536 | tf_op jit(solution)/shard_map/all_to_all | solution.py:130
  256.4 7.0 %copy-start.21 = (f32[64]{0:T(128)S(1)}, f32[64]{0:T(128)}, u32[]{:S(2)}) copy-start(f32[64]{0:T(128)} %param.12) | copy-start | bytes 772
  256.4 7.1 %copy-start.3 = (bf16[4096,256]{0,1:T(8,128)(2,1)S(1)}, bf16[4096,256]{0,1:T(8,128)(2,1)}, u32[]{:S(2)}) copy-start(bf16[4096,256]{0,1:T(8,128)(2,1)} %copy.81) | copy-start | bytes 6291460
  256.4 54.5 %all-to-all-start.3 = ((f32[16,256,128]{2,1,0:T(8,128)}), f32[16,256,128]{2,1,0:T(8,128)}, u32[]{:S(2)}, u32[]{:S(2)}) async-start(f32[16,256,128]{2,1,0:T(8,128)} %bitcast.183), calls=%async_computation.3 | async-start | bytes 4194304 | tf_op jit(solution)/shard_map/all_to_all | solution.py:141
  310.8 52.3 %all-to-all-start.2 = ((bf16[16,256,256]{1,2,0:T(8,128)(2,1)}), bf16[16,256,256]{1,2,0:T(8,128)(2,1)S(1)}, u32[]{:S(2)}, u32[]{:S(2)}) async-start(bf16[16,256,256]{1,2,0:T(8,128)(2,1)} %copy.92), calls=%async_computation.2 | async-start | bytes 4194304 | tf_op jit(solution)/shard_map/all_to_all | solution.py:127
  317.2 48.8 %collective-permute-start.2 = (f32[256,128]{1,0:T(8,128)S(1)}, f32[256,128]{1,0:T(8,128)S(1)}, u32[]{:S(2)}, u32[]{:S(2)}) collective-permute-start(f32[256,128]{1,0:T(8,128)S(1)} %reduce_sum.107), channel_id=1, source_target_pairs={{0,1},{1,0},{2,3},{3,2},{4,5},{5,4},{6,7},{7,6},{8,9},{9,8},{10,11... | collective-permute-start | bytes 393224 | tf_op jit(solution)/shard_map/ppermute | solution.py:143
  (7 other events, 16.6 us)
where the time goes:
time: 371 us; the launch traced here: 367 us
  waiting for transfers between devices  194 us (52%)
  matrix products  79.6 us (21%)
  local copies, waits for them, and re-layouts  43.8 us (12%)
  starting transfers between devices  32.2 us (9%)
  other arithmetic  15.8 us (4%)
    all_to_all x1, waiting for transfers between devices, local(): lax.all_to_all(xg, 'ctx', split_axis=1, concat_axis=0, tiled=True)  114 us
    all_to_all x1, waiting for transfers between devices, local(): lax.all_to_all(x_back, 'ctx', split_axis=0, concat_axis=1, tiled=True)  45.2 us
    all_to_all x1, waiting for transfers between devices, local(): lax.all_to_all(mine.reshape(owners, rows, state), 'ctx', split_axis=0, co...  32.7 us
    dot_general x2, matrix products, head_forward(): output = jnp.einsum('kij,kjp->kip', scores, x_blocks, precision=precise)  27.2 us
    dot_general x3, matrix products, head_forward(): states = jnp.einsum('kjp,kjn->kpn', weighted, b_blocks, precision=precise)  15.4 us
    unnamed x53, local copies, waits for them, and re-layouts  13.4 us
    dot_general x2, matrix products, head_forward(): jnp.einsum('kin,kpn->kip', reading, entering, precision=precise)  12.6 us
    dot_general x3, matrix products, head_forward(): jnp.einsum('kin,kjn->kij', c_blocks, b_blocks, precision=precise)  11.5 us
  transfers between devices with their start and end apart: 8, of which 4 were waited for; matrix products, arithmetic and copies ran while one was open for 15% of the time, Pallas kernels for 0%

commit v1 on v0

--- a/solution.py
+++ b/solution.py
@@ -81,6 +81,19 @@
     return x_back, raw_back, grad_b_all, grad_c_all
 
 
+def gather_ctx(block, owners, me):
+    if owners & (owners - 1):
+        return lax.all_gather(block, "ctx", axis=0, tiled=True)
+    have = block
+    step = 1
+    while step < owners:
+        theirs = lax.ppermute(have, "ctx", [(k, k ^ step) for k in range(owners)])
+        upper = (me // step) % 2 == 1
+        have = jnp.where(upper, jnp.concatenate([theirs, have]), jnp.concatenate([have, theirs]))
+        step *= 2
+    return have
+
+
 def local(x_act, b_proj, c_proj, dt_raw, a_log, d_skip, grad_out):
     rows = x_act.shape[0]
     heads_here = dt_raw.shape[1]
@@ -93,6 +106,10 @@
     me = lax.axis_index("ctx")
     half = lax.axis_index("tp")
 
+    own_seq = gather_ctx(jnp.where(half == 0, b_proj, c_proj), owners, me)
+    other_seq = lax.ppermute(own_seq, "tp", [(0, 1), (1, 0)])
+    b_rows = jnp.where(half == 0, own_seq, other_seq).astype(jnp.float32)
+    c_rows = jnp.where(half == 0, other_seq, own_seq).astype(jnp.float32)
     first_head = me * per_owner
     rate_own = lax.dynamic_slice_in_dim(a_log, first_head, per_owner)
     gain_own = lax.dynamic_slice_in_dim(d_skip, first_head, per_owner)
@@ -107,16 +124,8 @@
         sl = slice(c * per_chunk, (c + 1) * per_chunk)
         width = per_chunk * head_width
         pieces = [x4[:, :, sl, :].reshape(rows, owners, width), g4[:, :, sl, :].reshape(rows, owners, width)]
-        if c == 0:
-            own_proj = jnp.where(half == 0, b_proj, c_proj)
-            pieces.append(jnp.broadcast_to(own_proj[:, None, :], (rows, owners, state)))
         xg = jnp.concatenate(pieces, axis=2)
         xg_seq = lax.all_to_all(xg, "ctx", split_axis=1, concat_axis=0, tiled=True).reshape(rows * owners, -1)
-        if c == 0:
-            own_seq = xg_seq[:, 2 * width :]
-            other_seq = lax.ppermute(own_seq, "tp", [(0, 1), (1, 0)])
-            b_rows = jnp.where(half == 0, own_seq, other_seq).astype(jnp.float32)
-            c_rows = jnp.where(half == 0, other_seq, own_seq).astype(jnp.float32)
         raw_seq = lax.all_to_all(r3[:, :, sl], "ctx", split_axis=1, concat_axis=0, tiled=True).reshape(
             rows * owners, per_chunk
         )

time: 371 us -> 366 us (0.987)
  starting transfers between devices: 32.2 us -> 40.3 us
  local copies, waits for them, and re-layouts: 43.8 us -> 36.4 us
  waiting for transfers between devices: 194 us -> 188 us
    all_to_all x1, waiting for transfers between devices: 114 us -> 0.01 us  [local(): lax.all_to_all(xg, 'ctx', split_axis=1, concat_axis=0, tiled=True)]
    ppermute x0 -> x4, waiting for transfers between devices: none -> 107 us  [gather_ctx(): theirs = lax.ppermute(have, 'ctx', [(k, k ^ step) for k in range(owners)])]
    ppermute x0 -> x4, starting transfers between devices: none -> 5.2 us  [gather_ctx(): theirs = lax.ppermute(have, 'ctx', [(k, k ^ step) for k in range(owners)])]
    unnamed x53 -> x61, local copies, waits for them, and re-layouts: 13.4 us -> 11.7 us
  transfers between devices with their start and end apart: 8 -> 12, of which waited for: 4 -> 8; matrix products, arithmetic and copies ran while one was open for 15% -> 13% of each run, Pallas kernels for 0% -> 0%
where the time goes in v1:
time: 366 us; the launch traced here: 360 us
  waiting for transfers between devices  188 us (51%)
  matrix products  82.4 us (23%)
  starting transfers between devices  40.3 us (11%)
  local copies, waits for them, and re-layouts  36.4 us (10%)
  other arithmetic  12.5 us (3%)
    ppermute x4, waiting for transfers between devices, gather_ctx(): theirs = lax.ppermute(have, 'ctx', [(k, k ^ step) for k in range(owners)])  107 us
    all_to_all x1, waiting for transfers between devices, local(): lax.all_to_all(x_back, 'ctx', split_axis=0, concat_axis=1, tiled=True)  45.2 us
    all_to_all x1, waiting for transfers between devices, local(): lax.all_to_all(mine.reshape(owners, rows, state), 'ctx', split_axis=0, co...  33 us
    dot_general x2, matrix products, head_forward(): output = jnp.einsum('kij,kjp->kip', scores, x_blocks, precision=precise)  27.3 us
    dot_general x3, matrix products, head_forward(): states = jnp.einsum('kjp,kjn->kpn', weighted, b_blocks, precision=precise)  15.4 us
    dot_general x2, matrix products, head_forward(): jnp.einsum('kin,kpn->kip', reading, entering, precision=precise)  14.7 us
    dot_general x3, matrix products, head_forward(): jnp.einsum('kin,kjn->kij', c_blocks, b_blocks, precision=precise)  12.1 us
    unnamed x61, local copies, waits for them, and re-layouts  11.7 us
  transfers between devices with their start and end apart: 12, of which 8 were waited for; matrix products, arithmetic and copies ran while one was open for 13% of the time, Pallas kernels for 0%

profile of v1, /device:TPU:12, one launch (start us, length us, event | category | flops | bytes accessed | tf_op | source)
XLA Modules:
  0.0 360.5 jit_solution(3758670770003872119)
XLA Ops:
  2.0 7.2 %all-to-all-start.1 = ((bf16[256,16,4]{0,2,1:T(4,128)(2,1)}), bf16[256,16,4]{0,2,1:T(4,128)(2,1)S(1)}, u32[]{:S(2)}, u32[]{:S(2)}) async-start(bf16[256,16,4]{0,2,1:T(4,128)(2,1)} %reshape.131), calls=%async_computation.1 | async-start | bytes 65536 | tf_op jit(solution)/shard_map/all_to_all | solution.py:129
  12.5 4.1 %copy.77 = bf16[256,4096]{0,1:T(8,128)(2,1)} copy(bf16[256,4096]{1,0:T(8,128)(2,1)} %param.13) | data formatting | bytes 4194304 | tf_op args[6]
  16.5 3.9 %pad_maximum_fusion = bf16[256,16,512]{0,2,1:T(8,128)(2,1)} fusion(bf16[256,16,256]{0,2,1:T(8,128)(2,1)} %bitcast.186, bf16[256,16,256]{0,2,1:T(8,128)(2,1)S(1)} %bitcast.185), kind=kLoop, calls=%fused_computation.19 | loop fusion | flops 8388608 | bytes 8388608 | tf_op jit(solution)/shard_map/concatenate | solution.py:127
  20.4 7.1 %all-to-all-start = ((bf16[256,16,512]{0,2,1:T(8,128)(2,1)}), bf16[256,16,512]{0,2,1:T(8,128)(2,1)}, u32[]{:S(2)}, u32[]{:S(2)}) async-start(bf16[256,16,512]{0,2,1:T(8,128)(2,1)} %pad_maximum_fusion), calls=%async_computation | async-start | bytes 8388608 | tf_op jit(solution)/shard_map/all_to_all | solution.py:128
  29.1 12.3 %collective-permute-done = bf16[256,128]{1,0:T(8,128)(2,1)S(1)} collective-permute-done((bf16[256,128]{1,0:T(8,128)(2,1)S(1)}, bf16[256,128]{1,0:T(8,128)(2,1)S(1)}, u32[]{:S(2)}, u32[]{:S(2)}) %collective-permute-start) | collective-permute-done | bytes 65568 | tf_op jit(solution)/shard_map/ppermute | solution.py:90
  42.1 10.0 %collective-permute-done.1 = bf16[512,128]{1,0:T(8,128)(2,1)S(1)} collective-permute-done((bf16[512,128]{1,0:T(8,128)(2,1)S(1)}, bf16[512,128]{1,0:T(8,128)(2,1)S(1)}, u32[]{:S(2)}, u32[]{:S(2)}) %collective-permute-start.1) | collective-permute-done | bytes 131104 | tf_op jit(solution)/shard_map/ppermute | solution.py:90
  53.5 48.6 %collective-permute-done.2 = bf16[1024,128]{1,0:T(8,128)(2,1)S(1)} collective-permute-done((bf16[1024,128]{1,0:T(8,128)(2,1)S(1)}, bf16[1024,128]{1,0:T(8,128)(2,1)S(1)}, u32[]{:S(2)}, u32[]{:S(2)}) %collective-permute-start.2) | collective-permute-done | bytes 262176 | tf_op jit(solution)/shard_map/ppermute | solution.py:90
  104.1 35.6 %collective-permute-done.3 = bf16[2048,128]{1,0:T(8,128)(2,1)S(1)} collective-permute-done((bf16[2048,128]{1,0:T(8,128)(2,1)S(1)}, bf16[2048,128]{1,0:T(8,128)(2,1)S(1)}, u32[]{:S(2)}, u32[]{:S(2)}) %collective-permute-start.3) | collective-permute-done | bytes 524320 | tf_op jit(solution)/shard_map/ppermute | solution.py:90
  147.2 6.5 %copy.78 = bf16[16,256,1,512]{3,1,0,2:T(8,128)(2,1)} copy(bf16[16,256,1,512]{1,3,0,2:T(8,128)(2,1)} %bitcast.3) | data formatting | bytes 8388608 | tf_op jit(solution)/shard_map/all_to_all | solution.py:128
  153.6 3.8 %fusion.112 = (bf16[4096,256]{1,0:T(8,128)(2,1)}, bf16[4096,256]{1,0:T(8,128)(2,1)S(1)}) fusion(bf16[4096,512]{1,0:T(8,128)(2,1)} %bitcast.176), kind=kLoop, calls=%fused_computation.136 | loop fusion | bytes 8388608 | tf_op jit(solution)/shard_map/slice | solution.py:133
  163.4 8.1 %multiply_reduce_fusion.4 = (f32[4,16]{1,0:T(4,128)}, f32[4,16,64,128]{3,2,1,0:T(8,128)S(1)}) fusion(f32[16,256,128]{1,2,0:T(8,128)} %copy.81, f32[4,16,256]{2,1,0:T(8,128)S(1)} %get-tuple-element.36, bf16[4,8,16,8,256]{4,3,2,1,0:T(8,128)(2,1)} %bitcast.171), kind=kOutput, calls=%fused_computation.41 | convolution fusion | flops 1613758464 | bytes 6357248 | tf_op jit(solution)/shard_map/transpose(jvp(vmap(kin,kpn->kip)))/dot_general | solution.py:51
  174.7 4.5 %fusion.10 = (f32[4,16,256]{2,0,1:T(4,128)S(1)}, f32[16,4,64,256]{3,2,1,0:T(8,128)}) fusion(bf16[4,8,16,8,256]{4,3,2,1,0:T(8,128)(2,1)S(1)} %bitcast.163, bf16[16,256,128,1]{2,1,3,0:T(8,128)(2,1)S(1)} %bitcast.168, f32[16,4,64,128]{3,0,2,1:T(8,128)S(1)} %fusion.44), kind=kOutput, calls=%fused_computation.18 | convolution fusion | flops 1613742080 | bytes 9502720 | tf_op jit(solution)/shard_map/transpose(jvp(vmap(kjp,kjn->kpn)))/dot_general | solution.py:38
  179.3 16.5 %fusion.5 = (f32[4,16,256]{2,1,0:T(8,128)}, f32[4,16,256]{2,1,0:T(8,128)}, f32[4,16,256]{2,1,0:T(8,128)S(1)}, f32[16,256,256]{2,1,0:T(8,128)}, f32[4,16,256,256]{3,2,1,0:T(8,128)}) fusion(f32[4,16,256]{2,1,0:T(8,128)S(1)} %bitcast.196, f32[4,16,256]{2,1,0:T(8,128)S(1)} %get-tuple-element.37, f32[16,256,256]{2,1,0:T(8,128)S(1)} %copy-done.10, ...), kind=kOutput, calls=%fused_computation.9 | convolution fusion | flops 594493440 | bytes 29753344 | tf_op jit(solution)/shard_map/transpose(jvp(vmap(kij,kjp->kip)))/dot_general | solution.py:35
  198.8 8.6 %fusion.9 = f32[16,256,128,1]{2,1,3,0:T(8,128)} fusion(f32[4,16,256]{2,0,1:T(4,128)S(1)} %copy.80, f32[16,4,64,128]{3,0,2,1:T(8,128)S(1)} %fusion.44, bf16[4,8,16,8,256]{4,3,2,1,0:T(8,128)(2,1)S(1)} %bitcast.166), kind=kOutput, calls=%fused_computation.17 | convolution fusion | flops 1612709888 | bytes 6356992 | tf_op jit(solution)/shard_map/transpose(jvp(vmap(kjp,kjn->kpn)))/dot_general | solution.py:38
  210.5 6.6 %multiply_reduce_fusion.2 = (f32[4,16,256]{2,1,0:T(8,128)}, f32[16,256,128]{1,2,0:T(8,128)}) fusion(f32[16,256,128]{1,2,0:T(8,128)S(1)} %copy-done.11, f32[4,16,256]{2,1,0:T(8,128)S(1)} %copy-done.15, f32[4,16,64,128]{3,1,2,0:T(8,128)S(1)} %fusion.47, bf16[4,8,16,8,256]{4,3,2,1,0:T(8,128)(2,1)S(1)} %bitcast.173), kind=kOutput, calls=%fused_computation.10 | convolution fusion | flops 1618460672 | bytes 8519680 | tf_op jit(solution)/shard_map/transpose(jvp(vmap(kin,kpn->kip)))/dot_general | solution.py:51
  219.1 4.5 %convolution_add_fusion = f32[16,256,128]{2,1,0:T(8,128)S(1)} fusion(f32[16,256,128]{2,1,0:T(8,128)S(1)} %copy.100, f32[16,256,256]{2,1,0:T(8,128)} %get-tuple-element.15, bf16[16,256,128]{2,1,0:T(8,128)(2,1)S(1)} %bitcast.170), kind=kOutput, calls=%fused_computation.56 | convolution fusion | flops 1611137024 | bytes 9437184 | tf_op jit(solution)/shard_map/transpose(jvp(vmap(kin,kjn->kij)))/dot_general | solution.py:31
  223.6 4.9 %broadcast_select_fusion.1 = (f32[16,256,128]{2,1,0:T(8,128)S(1)}, f32[16,256,128]{2,1,0:T(8,128)}) fusion(f32[16,256,128]{2,1,0:T(8,128)S(1)} %convolution_add_fusion, pred[]{:T(512)S(6)} %eq.31, f32[16,256,256]{2,1,0:T(8,128)S(1)} %copy-done.4, bf16[16,256,128]{2,1,0:T(8,128)(2,1)S(1)} %bitcast.180, f32[16,256,128,1]{2,1,3,0:T(8,128)S(1)} %copy-done.9), kind=kOutput, calls=%fused_computation.71 | convolution fusion | flops 1612185600 | bytes 13631489 | tf_op jit(solution)/shard_map/transpose(jvp(vmap(kin,kjn->kij)))/dot_general | solution.py:31
  228.8 5.3 %fusion.111 = (f32[4,16]{1,0:T(4,128)S(1)}, f32[4,16]{1,0:T(4,128)S(1)}) fusion(f32[4,16]{1,0:T(4,128)S(1)} %get-tuple-element.38, f32[4,16]{1,0:T(4,128)S(1)} %get-tuple-element.21, f32[16,4,64,128]{3,2,1,0:T(8,128)S(1)} %copy-done.1, f32[4,16,64,128]{3,2,1,0:T(8,128)S(1)} %copy-done.8, pred[16,16]{1,0:T(8,128)(4,1)S(1)} %iota_compare_fusion.6), kind=kOutput, calls=%fused_computation.135 | convolution fusion | flops 100669312 | bytes 4195584 | tf_op jit(solution)/shard_map/transpose(jvp(vmap(kj,jpn->kpn)))/dot_general | solution.py:47
  235.4 8.9 %all-to-all-start.4 = ((bf16[16,256,4]{1,2,0:T(4,128)(2,1)}), bf16[16,256,4]{1,2,0:T(4,128)(2,1)S(1)}, u32[]{:S(2)}, u32[]{:S(2)}) async-start(bf16[16,256,4]{1,2,0:T(4,128)(2,1)} %bitcast.41), calls=%async_computation.4 | async-start | bytes 65536 | tf_op jit(solution)/shard_map/all_to_all | solution.py:139
  249.5 7.0 %all-to-all-start.3 = ((f32[16,256,128]{2,1,0:T(8,128)}), f32[16,256,128]{2,1,0:T(8,128)}, u32[]{:S(2)}, u32[]{:S(2)}) async-start(f32[16,256,128]{2,1,0:T(8,128)} %bitcast.181), calls=%async_computation.3 | async-start | bytes 4194304 | tf_op jit(solution)/shard_map/all_to_all | solution.py:150
  256.6 10.8 %fusion.12 = f32[16,4,8,8,256]{4,3,2,1,0:T(8,128)S(1)} fusion(f32[16,4,64,256]{3,2,1,0:T(8,128)} %get-tuple-element.40, f32[4,16,256]{2,0,1:T(4,128)S(1)} %copy.80, bf16[4,8,16,8,256]{4,3,2,1,0:T(8,128)(2,1)S(1)} %bitcast.174, f32[4,16,256,256]{3,2,1,0:T(8,128)} %get-tuple-element.22), kind=kOutput, calls=%fused_computation.22 | convolution fusion | flops 3223322624 | bytes 27328512 | tf_op jit(solution)/shard_map/transpose(jvp(vmap(kij,kjp->kip)))/dot_general | solution.py:35
  271.3 33.0 %all-to-all-done.3 = f32[16,256,128]{2,1,0:T(8,128)} async-done(((f32[16,256,128]{2,1,0:T(8,128)}), f32[16,256,128]{2,1,0:T(8,128)}, u32[]{:S(2)}, u32[]{:S(2)}) %all-to-all-start.3) | async-done | bytes 2097184 | tf_op jit(solution)/shard_map/all_to_all | solution.py:150
  304.3 4.7 %all-to-all-start.2 = ((bf16[16,256,256]{1,2,0:T(8,128)(2,1)}), bf16[16,256,256]{1,2,0:T(8,128)(2,1)S(1)}, u32[]{:S(2)}, u32[]{:S(2)}) async-start(bf16[16,256,256]{1,2,0:T(8,128)(2,1)} %copy.90), calls=%async_computation.2 | async-start | bytes 4194304 | tf_op jit(solution)/shard_map/all_to_all | solution.py:136
  311.4 45.2 %all-to-all-done.2 = bf16[16,256,256]{1,2,0:T(8,128)(2,1)S(1)} async-done(((bf16[16,256,256]{1,2,0:T(8,128)(2,1)}), bf16[16,256,256]{1,2,0:T(8,128)(2,1)S(1)}, u32[]{:S(2)}, u32[]{:S(2)}) %all-to-all-start.2) | async-done | bytes 2097184 | tf_op jit(solution)/shard_map/all_to_all | solution.py:136
  (110 shorter events, 51.6 us)
Async XLA Ops:
  2.0 18.4 %all-to-all-start.1 = ((bf16[256,16,4]{0,2,1:T(4,128)(2,1)}), bf16[256,16,4]{0,2,1:T(4,128)(2,1)S(1)}, u32[]{:S(2)}, u32[]{:S(2)}) async-start(bf16[256,16,4]{0,2,1:T(4,128)(2,1)} %reshape.131), calls=%async_computation.1 | async-start | bytes 65536 | tf_op jit(solution)/shard_map/all_to_all | solution.py:129
  20.4 7.1 %copy-start.12 = (bf16[256,128]{1,0:T(8,128)(2,1)S(1)}, bf16[256,128]{1,0:T(8,128)(2,1)}, u32[]{:S(2)}) copy-start(bf16[256,128]{1,0:T(8,128)(2,1)} %param.8) | copy-start | bytes 196612
  20.4 7.1 %copy-start.13 = (bf16[256,128]{1,0:T(8,128)(2,1)S(1)}, bf16[256,128]{1,0:T(8,128)(2,1)}, u32[]{:S(2)}) copy-start(bf16[256,128]{1,0:T(8,128)(2,1)} %param.9) | copy-start | bytes 196612
  20.4 126.7 %all-to-all-start = ((bf16[256,16,512]{0,2,1:T(8,128)(2,1)}), bf16[256,16,512]{0,2,1:T(8,128)(2,1)}, u32[]{:S(2)}, u32[]{:S(2)}) async-start(bf16[256,16,512]{0,2,1:T(8,128)(2,1)} %pad_maximum_fusion), calls=%async_computation | async-start | bytes 8388608 | tf_op jit(solution)/shard_map/all_to_all | solution.py:128
  27.5 76.4 %copy-start.24 = (f32[64]{0:T(128)S(1)}, f32[64]{0:T(128)}, u32[]{:S(2)}) copy-start(f32[64]{0:T(128)} %param.11) | copy-start | bytes 772
  27.6 13.9 %collective-permute-start = (bf16[256,128]{1,0:T(8,128)(2,1)S(1)}, bf16[256,128]{1,0:T(8,128)(2,1)S(1)}, u32[]{:S(2)}, u32[]{:S(2)}) collective-permute-start(bf16[256,128]{1,0:T(8,128)(2,1)S(1)} %broadcast_select_fusion.6), channel_id=1, source_target_pairs={{0,2},{2,0},{4,6},{6,4},{8,10},{10,8},{12,14},{14,12},{16,18},{18,... | collective-permute-start | bytes 196616 | tf_op jit(solution)/shard_map/ppermute | solution.py:90
  41.5 10.7 %collective-permute-start.1 = (bf16[512,128]{1,0:T(8,128)(2,1)S(1)}, bf16[512,128]{1,0:T(8,128)(2,1)S(1)}, u32[]{:S(2)}, u32[]{:S(2)}) collective-permute-start(bf16[512,128]{1,0:T(8,128)(2,1)S(1)} %maximum_select_fusion.3), channel_id=1, source_target_pairs={{0,4},{2,6},{4,0},{6,2},{8,12},{10,14},{12,8},{14,10},{16,20},{18,... | collective-permute-start | bytes 393224 | tf_op jit(solution)/shard_map/ppermute | solution.py:90
  52.2 49.8 %collective-permute-start.2 = (bf16[1024,128]{1,0:T(8,128)(2,1)S(1)}, bf16[1024,128]{1,0:T(8,128)(2,1)S(1)}, u32[]{:S(2)}, u32[]{:S(2)}) collective-permute-start(bf16[1024,128]{1,0:T(8,128)(2,1)S(1)} %maximum_select_fusion.2), channel_id=1, source_target_pairs={{0,8},{2,10},{4,12},{6,14},{8,0},{10,2},{12,4},{14,6},{16,24},{18,... | collective-permute-start | bytes 786440 | tf_op jit(solution)/shard_map/ppermute | solution.py:90
  102.2 37.5 %collective-permute-start.3 = (bf16[2048,128]{1,0:T(8,128)(2,1)S(1)}, bf16[2048,128]{1,0:T(8,128)(2,1)S(1)}, u32[]{:S(2)}, u32[]{:S(2)}) collective-permute-start(bf16[2048,128]{1,0:T(8,128)(2,1)S(1)} %maximum_select_fusion.1), channel_id=1, source_target_pairs={{0,16},{2,18},{4,20},{6,22},{8,24},{10,26},{12,28},{14,30},{16,0},... | collective-permute-start | bytes 1572872 | tf_op jit(solution)/shard_map/ppermute | solution.py:90
  104.0 36.7 %copy-start.22 = (f32[4]{0:T(128)}, f32[4]{0:T(128)S(1)}, u32[]{:S(2)}) copy-start(f32[4]{0:T(128)S(1)} %exponential_negate_fusion) | copy-start | bytes 52
  139.9 2.7 collective-permute-start.4
  141.0 22.4 %copy-start.14 = (f32[4,16,256]{2,1,0:T(8,128)}, f32[4,16,256]{2,1,0:T(8,128)S(1)}, u32[]{:S(2)}) copy-start(f32[4,16,256]{2,1,0:T(8,128)S(1)} %get-tuple-element.36) | copy-start | bytes 196612
  198.8 8.6 %copy-start = (f32[16,4,64,128]{3,2,1,0:T(8,128)}, f32[16,4,64,128]{3,2,1,0:T(8,128)S(1)}, u32[]{:S(2)}) copy-start(f32[16,4,64,128]{3,2,1,0:T(8,128)S(1)} %fusion.8) | copy-start | bytes 6291460
  198.8 8.6 %copy-start.20 = (f32[4,16]{1,0:T(4,128)S(1)}, f32[4,16]{1,0:T(4,128)}, u32[]{:S(2)}) copy-start(f32[4,16]{1,0:T(4,128)} %get-tuple-element.20) | copy-start | bytes 772
  228.5 5.8 %copy-start.17 = (f32[4,16,256]{2,1,0:T(8,128)S(1)}, f32[4,16,256]{2,1,0:T(8,128)}, u32[]{:S(2)}) copy-start(f32[4,16,256]{2,1,0:T(8,128)} %get-tuple-element.13) | copy-start | bytes 196612
  228.5 5.8 %copy-start.18 = (f32[4,16,256]{2,1,0:T(8,128)S(1)}, f32[4,16,256]{2,1,0:T(8,128)}, u32[]{:S(2)}) copy-start(f32[4,16,256]{2,1,0:T(8,128)} %get-tuple-element.16) | copy-start | bytes 196612
  228.5 6.1 %copy-start.23 = (f32[4]{0:T(128)S(1)}, f32[4]{0:T(128)}, u32[]{:S(2)}) copy-start(f32[4]{0:T(128)} %copy-done.22) | copy-start | bytes 52
  228.6 15.7 %collective-permute-start.5 = (f32[4096,128]{1,0:T(8,128)}, f32[4096,128]{1,0:T(8,128)}, u32[]{:S(2)}, u32[]{:S(2)}) collective-permute-start(f32[4096,128]{1,0:T(8,128)} %bitcast.35), channel_id=1, source_target_pairs={{0,1},{1,0},{2,3},{3,2},{4,5},{5,4},{6,7},{7,6},{8,9},{9,8},{10,11... | collective-permute-start | bytes 6291464 | tf_op jit(solution)/shard_map/ppermute | solution.py:149
  235.4 14.1 %all-to-all-start.4 = ((bf16[16,256,4]{1,2,0:T(4,128)(2,1)}), bf16[16,256,4]{1,2,0:T(4,128)(2,1)S(1)}, u32[]{:S(2)}, u32[]{:S(2)}) async-start(bf16[16,256,4]{1,2,0:T(4,128)(2,1)} %bitcast.41), calls=%async_computation.4 | async-start | bytes 65536 | tf_op jit(solution)/shard_map/all_to_all | solution.py:139
  249.5 7.0 %copy-start.25 = (f32[64]{0:T(128)S(1)}, f32[64]{0:T(128)}, u32[]{:S(2)}) copy-start(f32[64]{0:T(128)} %param.12) | copy-start | bytes 772
  249.5 7.1 %copy-start.3 = (bf16[4096,256]{0,1:T(8,128)(2,1)S(1)}, bf16[4096,256]{0,1:T(8,128)(2,1)}, u32[]{:S(2)}) copy-start(bf16[4096,256]{0,1:T(8,128)(2,1)} %copy.79) | copy-start | bytes 6291460
  249.5 54.8 %all-to-all-start.3 = ((f32[16,256,128]{2,1,0:T(8,128)}), f32[16,256,128]{2,1,0:T(8,128)}, u32[]{:S(2)}, u32[]{:S(2)}) async-start(f32[16,256,128]{2,1,0:T(8,128)} %bitcast.181), calls=%async_computation.3 | async-start | bytes 4194304 | tf_op jit(solution)/shard_map/all_to_all | solution.py:150
  304.3 52.4 %all-to-all-start.2 = ((bf16[16,256,256]{1,2,0:T(8,128)(2,1)}), bf16[16,256,256]{1,2,0:T(8,128)(2,1)S(1)}, u32[]{:S(2)}, u32[]{:S(2)}) async-start(bf16[16,256,256]{1,2,0:T(8,128)(2,1)} %copy.90), calls=%async_computation.2 | async-start | bytes 4194304 | tf_op jit(solution)/shard_map/all_to_all | solution.py:136
  310.7 48.8 %collective-permute-start.6 = (f32[256,128]{1,0:T(8,128)S(1)}, f32[256,128]{1,0:T(8,128)S(1)}, u32[]{:S(2)}, u32[]{:S(2)}) collective-permute-start(f32[256,128]{1,0:T(8,128)S(1)} %reduce_sum.107), channel_id=1, source_target_pairs={{0,1},{1,0},{2,3},{3,2},{4,5},{5,4},{6,7},{7,6},{8,9},{9,8},{10,11... | collective-permute-start | bytes 393224 | tf_op jit(solution)/shard_map/ppermute | solution.py:152
  (15 other events, 67.9 us)
